TPU v7x, 256 devices: a whole 4x4x8 slice. The times are simulated.
256 devices in a mesh: gx: 16 (over z, core), gy: 16 (over x, y).
Axes of the slice: x: 4, y: 4, z: 8, core: 2. Of those that a mesh axis runs over, the one named last changes fastest.
Arguments:
- state: bfloat16 [2, 256, 768, 2048], P(None, None, 'gx', 'gy'), as said below
Outputs:
- modes: bfloat16 [255, 2, 768, 2048], P(None, None, 'gx', 'gy')
- reduced: float32 [255, 255], replicated
Inputs may be any that keep to these rules, and one draw needn't show every extreme that they name: `state`: both fields are positive.
All inputs are finite; a program needn't handle non-finite values.
Results may differ from a plain program's by a relative error of at most 0.0077.
Values may be sent and summed in bfloat16 or wider, within the bound.
No kernel may reach another device: no remote copies, remote signals or barrier semaphores. Data moves between devices by JAX's collectives and lax.ppermute only.
A program may use at most 128 MiB of HBM per device.

v0:
```python
import jax
import jax.numpy as jnp
from jax import lax
from jax.sharding import PartitionSpec as P


def padded_2(cells, sides, width):
    for axis, dim in sides:
        count = lax.axis_size(axis)
        ends = count - 1
        head = lax.slice_in_dim(cells, 0, width, axis=dim)
        tail = lax.slice_in_dim(cells, cells.shape[dim] - width, cells.shape[dim], axis=dim)
        cells = jnp.concatenate(
            [
                lax.ppermute(tail, axis, [(i, (i + 1) % count) for i in range(ends)]),
                cells,
                lax.ppermute(head, axis, [((i + 1) % count, i) for i in range(ends)]),
            ],
            axis=dim,
        )
    return cells


def tri_solve(lower, right):
    return lax.linalg.triangular_solve(lower, right, left_side=True, lower=True)


def gradients(padded):
    grad_x = (
        padded[:, :-4, 2:-2]
        - 8.0 * padded[:, 1:-3, 2:-2]
        + 8.0 * padded[:, 3:-1, 2:-2]
        - padded[:, 4:, 2:-2]
    ) / 12.0
    grad_y = (
        padded[:, 2:-2, :-4]
        - 8.0 * padded[:, 2:-2, 1:-3]
        + 8.0 * padded[:, 2:-2, 3:-1]
        - padded[:, 2:-2, 4:]
    ) / 12.0
    return jnp.stack([grad_x, grad_y], axis=1).astype(jnp.bfloat16)


def shards(state):
    snaps = state.shape[1]
    rows_x = state.shape[2]
    rows_y = state.shape[3]
    total_rows = 2 * rows_x * rows_y * lax.axis_size("gx") * lax.axis_size("gy")
    temp = 0.4 * state[1].astype(jnp.float32) / state[0].astype(jnp.float32)
    padded = padded_2(temp, (("gx", 1), ("gy", 2)), 2)
    features = gradients(padded)
    snap = features.reshape(snaps, 2 * rows_x * rows_y)
    local_gram = (
        lax.dot_general(snap, snap, (((1,), (1,)), ((), ())), preferred_element_type=jnp.float32)
        / total_rows
    )
    gram = lax.psum(local_gram, ("gx", "gy"))
    lower = jnp.linalg.cholesky(gram[: snaps - 1, : snaps - 1])
    cross = gram[: snaps - 1, 1:]
    half = tri_solve(lower, cross)
    reduced = tri_solve(lower, half.T).T
    inverse = tri_solve(lower, jnp.eye(snaps - 1, dtype=jnp.float32)).astype(jnp.bfloat16)
    modes = jnp.dot(inverse, snap[1:], preferred_element_type=jnp.float32).astype(jnp.bfloat16)
    return (modes.reshape(snaps - 1, 2, rows_x, rows_y), reduced)


def solution(mesh):
    placed = (P(None, None, "gx", "gy"),)
    return jax.shard_map(
        shards,
        mesh=mesh,
        in_specs=placed,
        out_specs=(P(None, None, "gx", "gy"), P()),
        check_vma=False,
    )
```

profile of v0, /device:TPU:2, one launch (start us, length us, event | category | flops | bytes accessed | tf_op | source)
XLA Modules:
  0.0 435.9 jit_solution(15575594914575890213)
XLA Ops:
  7.2 3.9 fusion.44
  11.1 1.3 divide_bitcast_fusion
  12.5 1.8 collective-permute-start
  14.3 1.3 collective-permute-start.1
  16.3 3.1 collective-permute-done.1
  20.1 3.6 pad_maximum_fusion.1
  23.7 11.6 %fusion.42 = (f32[256,52,2]{2,0,1:T(8,128)}, f32[256,52,2]{2,0,1:T(8,128)}) fusion(f32[256,52,128]{2,0,1:T(8,128)} %pad_maximum_fusion.1), kind=kLoop, calls=%fused_computation.88 | loop fusion | bytes 425984 | tf_op jit(solution)/shard_map/slice | solution.py:12
  35.4 4.7 %copy.16 = f32[256,52,2]{0,2,1:T(2,128)S(1)} copy(f32[256,52,2]{2,0,1:T(8,128)} %get-tuple-element.41) | data formatting | bytes 212992 | tf_op jit(solution)/shard_map/slice | solution.py:12
  40.1 3.5 collective-permute-start.2
  43.6 5.3 %copy.18 = f32[256,52,2]{0,2,1:T(2,128)} copy(f32[256,52,2]{2,0,1:T(8,128)} %get-tuple-element.42) | data formatting | bytes 212992 | tf_op jit(solution)/shard_map/slice | solution.py:11
  48.9 4.6 %collective-permute-start.3 = (f32[256,52,2]{0,2,1:T(2,128)}, f32[256,52,2]{0,2,1:T(2,128)}, u32[]{:S(2)}, u32[]{:S(2)}) collective-permute-start(f32[256,52,2]{0,2,1:T(2,128)} %copy.18), channel_id=1, source_target_pairs={{1,0},{2,1},{3,2},{4,3},{5,4},{6,5},{7,6},{8,7},{9,8},{10,9},{11,1... | collective-permute-start | bytes 319496 | tf_op jit(solution)/shard_map/ppermute | solution.py:17
  53.5 11.1 %fusion.17 = bf16[256,1,48,128]{3,0,2,1:T(8,128)(2,1)S(1)} fusion(f32[256,2,128]{2,0,1:T(8,128)} %copy-done.2, f32[256,48,128]{2,0,1:T(8,128)} %copy-done, f32[256,2,128]{2,0,1:T(8,128)S(1)} %collective-permute-done), kind=kLoop, calls=%fused_computation.36 | loop fusion | flops 17301504 | bytes 9961472 | tf_op jit(solution)/shard_map/stack | solution.py:41
  64.6 5.0 %copy.17 = f32[256,52,2]{2,0,1:T(8,128)} copy(f32[256,52,2]{0,2,1:T(2,128)} %collective-permute-done.2) | data formatting | bytes 212992 | tf_op jit(solution)/shard_map/ppermute | solution.py:15
  69.6 5.1 %copy.19 = f32[256,52,2]{2,0,1:T(8,128)} copy(f32[256,52,2]{0,2,1:T(2,128)} %collective-permute-done.3) | data formatting | bytes 212992 | tf_op jit(solution)/shard_map/ppermute | solution.py:17
  74.7 21.0 %fusion.18 = bf16[256,1,48,128]{3,0,2,1:T(8,128)(2,1)S(1)} fusion(f32[256,52,2]{2,0,1:T(8,128)} %copy.19, f32[256,2,128]{2,0,1:T(8,128)} %copy-done.2, f32[256,48,128]{2,0,1:T(8,128)} %copy-done, f32[256,2,128]{2,0,1:T(8,128)S(1)} %collective-permute-done, f32[256,52,2]{2,0,1:T(8,128)} %copy.17), kind=kLoop, calls=%fused_computation.37 | loop fusion | flops 29884416 | bytes 10174464 | tf_op jit(solution)/shard_map/stack | solution.py:41
  95.8 1.7 copy-done.1
  97.4 2.5 fusion.20
  100.0 5.9 %fusion.8 = bf16[255,2,48,128]{3,0,2,1:T(8,128)(2,1)} fusion(bf16[256,1,48,128]{3,0,2,1:T(8,128)(2,1)S(1)} %fusion.17, bf16[256,1,48,128]{3,0,2,1:T(8,128)(2,1)} %copy-done.1), kind=kLoop, calls=%fused_computation.17 | loop fusion | flops 3133440 | bytes 12558336 | tf_op jit(solution)/shard_map/stack | solution.py:41
  105.8 8.7 %copy.22 = bf16[255,2,48,128]{0,3,2,1:T(8,128)(2,1)} copy(bf16[255,2,48,128]{3,0,2,1:T(8,128)(2,1)} %fusion.8) | data formatting | bytes 12533760 | tf_op jit(solution)/shard_map/slice | solution.py:63
  114.5 240.5 %all-reduce.4.cloned.1.call-done = f32[256,256]{0,1:T(8,128)} async-done(((f32[256,256]{0,1:T(8,128)}), f32[256,256]{0,1:T(8,128)}) %all-reduce.4.cloned.1.call-update) | async-done | bytes 262160 | tf_op jit(solution)/shard_map/psum | solution.py:57
  355.0 1.1 copy.21
  356.1 1.0 fusion.21
  357.1 11.7 %cholesky.51 = f32[128,128]{1,0:T(8,128)S(1)} custom-call(f32[128,128]{1,0:T(8,128)S(1)} %cholesky.124), custom_call_target="Cholesky" | custom-call | tf_op jit(solution)/shard_map/jit(cholesky)/cholesky | solution.py:58
  368.9 9.8 %custom-call.14 = f32[1,128,128]{1,2,0:T(8,128)S(1)} custom-call(f32[1,128,128]{2,1,0:T(8,128)S(1)} %get-tuple-element.50), custom_call_target="InvertDiagBlocksLowerTriangular" | custom-call | tf_op jit(solution)/shard_map/jit(cholesky)/cholesky | solution.py:58
  379.2 11.6 %cholesky.110 = f32[127,127]{1,0:T(8,128)S(1)} custom-call(f32[127,127]{1,0:T(8,128)S(1)} %convolution_subtract_fusion.2), custom_call_target="Cholesky" | custom-call | tf_op jit(solution)/shard_map/jit(cholesky)/cholesky | solution.py:58
  393.6 19.9 %custom-call.17 = f32[2,128,128]{1,2,0:T(8,128)S(1)} custom-call(f32[2,128,128]{2,1,0:T(8,128)S(1)} %pad_maximum_fusion.15), custom_call_target="InvertDiagBlocksLowerTriangular" | custom-call | tf_op jit(solution)/shard_map/triangular_solve/custom-call.0 | solution.py:25
  413.5 1.2 fusion.26
  415.1 1.2 fusion.25
  417.4 0.8 copy.25
  419.2 4.6 %convolution_convert_fusion = bf16[255,12288]{1,0:T(8,128)(2,1)S(1)} fusion(bf16[255,12288]{0,1:T(8,128)(2,1)} %bitcast.61, bf16[127,255]{1,0:T(8,128)(2,1)S(1)} %fusion.35, f32[128,255]{1,0:T(8,128)S(1)} %fusion.28), kind=kOutput, calls=%fused_computation | convolution fusion | flops 1601447936 | bytes 12729090 | tf_op jit(solution)/shard_map/dot_general | solution.py:63
  423.8 1.5 copy.32
  425.3 3.8 slice.212
  (37 shorter events, 5.8 us)
Async XLA Ops:
  7.2 347.8 %all-reduce.4.cloned.1.call-start = ((), (), s32[]{:S(2)}) async-start(), calls=%async_computation | async-start | bytes 524288 | tf_op jit(solution)/shard_map/psum | solution.py:57
  12.5 6.9 %copy-start = (f32[256,48,128]{2,0,1:T(8,128)}, f32[256,48,128]{2,0,1:T(8,128)S(1)}, u32[]{:S(2)}) copy-start(f32[256,48,128]{2,0,1:T(8,128)S(1)} %divide_bitcast_fusion) | copy-start | bytes 18874372
  12.5 3.8 collective-permute-start
  14.3 5.1 %collective-permute-start.1 = (f32[256,2,128]{2,0,1:T(8,128)S(1)}, f32[256,2,128]{2,0,1:T(8,128)S(1)}, u32[]{:S(2)}, u32[]{:S(2)}) collective-permute-start(f32[256,2,128]{2,0,1:T(8,128)S(1)} %get-tuple-element.44), channel_id=1, source_target_pairs={{16,0},{32,16},{48,32},{64,48},{80,64},{96,80},{112,96},{128,112},... | collective-permute-start | bytes 786440 | tf_op jit(solution)/shard_map/ppermute | solution.py:17
  19.4 0.7 copy-start.2
  40.1 24.5 %collective-permute-start.2 = (f32[256,52,2]{0,2,1:T(2,128)S(1)}, f32[256,52,2]{0,2,1:T(2,128)}, u32[]{:S(2)}, u32[]{:S(2)}) collective-permute-start(f32[256,52,2]{0,2,1:T(2,128)S(1)} %copy.16), channel_id=1, source_target_pairs={{0,1},{1,2},{2,3},{3,4},{4,5},{5,6},{6,7},{7,8},{8,9},{9,10},{10,1... | collective-permute-start | bytes 319496 | tf_op jit(solution)/shard_map/ppermute | solution.py:15
  48.9 20.7 %collective-permute-start.3 = (f32[256,52,2]{0,2,1:T(2,128)}, f32[256,52,2]{0,2,1:T(2,128)}, u32[]{:S(2)}, u32[]{:S(2)}) collective-permute-start(f32[256,52,2]{0,2,1:T(2,128)} %copy.18), channel_id=1, source_target_pairs={{1,0},{2,1},{3,2},{4,3},{5,4},{6,5},{7,6},{8,7},{9,8},{10,9},{11,1... | collective-permute-start | bytes 319496 | tf_op jit(solution)/shard_map/ppermute | solution.py:17
  95.8 1.7 copy-start.1
  105.8 287.6 %copy-start.4 = (f32[128,1]{1,0:T(8,128)S(1)}, f32[128,1]{1,0:T(8,128)}, u32[]{:S(2)}) copy-start(f32[128,1]{1,0:T(8,128)} %constant.87.clone.3) | copy-start | bytes 1540
  114.5 303.8 %copy-start.3 = (f32[255,255]{1,0:T(8,128)S(1)}, f32[255,255]{1,0:T(8,128)}, u32[]{:S(2)}) copy-start(f32[255,255]{1,0:T(8,128)} %fusion.22) | copy-start | bytes 780304
Sparse Core Ops, SparseCore 0:
  100.1 254.8 all-reduce.3
where the time goes:
time: 437 us; the launch traced here: 436 us
  waiting for transfers between devices  244 us (56%)
  other arithmetic  99.2 us (23%)
  local copies, waits for them, and re-layouts  53.9 us (12%)
  between operations  15.6 us (4%)
  matrix products  12.3 us (3%)
  starting transfers between devices  11.2 us (3%)
    psum x1, waiting for transfers between devices, shards(): gram = lax.psum(local_gram, ('gx', 'gy'))  240 us
    another operation x3, other arithmetic, gradients(): return jnp.stack([grad_x, grad_y], axis=1).astype(jnp.bfloat16)  38 us
    another operation x7, other arithmetic, shards(): lower = jnp.linalg.cholesky(gram[:snaps - 1, :snaps - 1])  34.5 us
    another operation x4, other arithmetic, tri_solve(): return lax.linalg.triangular_solve(lower, right, left_side=True, lower=True)  20.1 us
    slice x3, local copies, waits for them, and re-layouts, padded_2(): lax.slice_in_dim(cells, cells.shape[dim] - width, cells.shape[dim], axis=...  16.4 us
  transfers between devices with their start and end apart: 5, of which 2 were waited for; matrix products, arithmetic and copies ran while one was open for 8% of the time, Pallas kernels for 0%

commit v1 on v0

--- a/solution.py
+++ b/solution.py
@@ -54,7 +54,7 @@
         lax.dot_general(snap, snap, (((1,), (1,)), ((), ())), preferred_element_type=jnp.float32)
         / total_rows
     )
-    gram = lax.psum(local_gram, ("gx", "gy"))
+    gram = lax.psum(lax.psum(local_gram, "gy"), "gx")
     lower = jnp.linalg.cholesky(gram[: snaps - 1, : snaps - 1])
     cross = gram[: snaps - 1, 1:]
     half = tri_solve(lower, cross)

time: 437 us -> 392 us (0.90)
  waiting for transfers between devices: 244 us -> 198 us
    psum x1 -> x2, waiting for transfers between devices: 240 us -> 194 us  [shards(): gram = lax.psum(lax.psum(local_gram, 'gy'), 'gx')]
  transfers between devices with their start and end apart: 5 -> 6, of which waited for: 2 -> 3; matrix products, arithmetic and copies ran while one was open for 8% -> 9% of each run, Pallas kernels for 0% -> 0%
where the time goes in v1:
time: 392 us; the launch traced here: 390 us
  waiting for transfers between devices  198 us (51%)
  other arithmetic  98.8 us (25%)
  local copies, waits for them, and re-layouts  53.9 us (14%)
  between operations  15.6 us (4%)
  matrix products  12.3 us (3%)
  starting transfers between devices  11.5 us (3%)
    psum x2, waiting for transfers between devices, shards(): gram = lax.psum(lax.psum(local_gram, 'gy'), 'gx')  194 us
    another operation x3, other arithmetic, gradients(): return jnp.stack([grad_x, grad_y], axis=1).astype(jnp.bfloat16)  38.2 us
    another operation x7, other arithmetic, shards(): lower = jnp.linalg.cholesky(gram[:snaps - 1, :snaps - 1])  34.5 us
    another operation x4, other arithmetic, tri_solve(): return lax.linalg.triangular_solve(lower, right, left_side=True, lower=True)  20.1 us
    slice x3, local copies, waits for them, and re-layouts, padded_2(): lax.slice_in_dim(cells, cells.shape[dim] - width, cells.shape[dim], axis=...  16.4 us
    slice x1, local copies, waits for them, and re-layouts, shards(): snap[1:]  8.66 us
    unnamed x11, local copies, waits for them, and re-layouts  8.44 us
  transfers between devices with their start and end apart: 6, of which 3 were waited for; matrix products, arithmetic and copies ran while one was open for 9% of the time, Pallas kernels for 0%

profile of v1, /device:TPU:2, one launch (start us, length us, event | category | flops | bytes accessed | tf_op | source)
XLA Modules:
  0.0 390.3 jit_solution(2503583490976444099)
XLA Ops:
  7.2 3.9 %fusion.43 = (bf16[1,256,48,128]{3,2,1,0:T(8,128)(2,1)S(1)}, bf16[1,256,48,128]{3,2,1,0:T(8,128)(2,1)S(1)}) fusion(bf16[2,256,48,128]{3,2,1,0:T(8,128)(2,1)} %param.3), kind=kLoop, calls=%fused_computation.89 | loop fusion | bytes 12582912 | tf_op jit(solution)/shard_map/slice | solution.py:49
  11.1 1.3 divide_bitcast_fusion
  12.5 1.8 collective-permute-start
  14.3 1.3 collective-permute-start.1
  15.6 3.8 collective-permute-done.1
  20.1 3.6 pad_maximum_fusion.1
  23.7 11.6 %fusion.41 = (f32[256,52,2]{2,0,1:T(8,128)}, f32[256,52,2]{2,0,1:T(8,128)}) fusion(f32[256,52,128]{2,0,1:T(8,128)} %pad_maximum_fusion.1), kind=kLoop, calls=%fused_computation.87 | loop fusion | bytes 425984 | tf_op jit(solution)/shard_map/slice | solution.py:12
  35.4 4.7 %copy.16 = f32[256,52,2]{0,2,1:T(2,128)S(1)} copy(f32[256,52,2]{2,0,1:T(8,128)} %get-tuple-element.41) | data formatting | bytes 212992 | tf_op jit(solution)/shard_map/slice | solution.py:12
  40.1 3.5 collective-permute-start.2
  43.6 5.3 %copy.18 = f32[256,52,2]{0,2,1:T(2,128)} copy(f32[256,52,2]{2,0,1:T(8,128)} %get-tuple-element.42) | data formatting | bytes 212992 | tf_op jit(solution)/shard_map/slice | solution.py:11
  48.9 4.6 %collective-permute-start.3 = (f32[256,52,2]{0,2,1:T(2,128)}, f32[256,52,2]{0,2,1:T(2,128)}, u32[]{:S(2)}, u32[]{:S(2)}) collective-permute-start(f32[256,52,2]{0,2,1:T(2,128)} %copy.18), channel_id=1, source_target_pairs={{1,0},{2,1},{3,2},{4,3},{5,4},{6,5},{7,6},{8,7},{9,8},{10,9},{11,1... | collective-permute-start | bytes 319496 | tf_op jit(solution)/shard_map/ppermute | solution.py:17
  53.5 11.1 %fusion.17 = bf16[256,1,48,128]{3,0,2,1:T(8,128)(2,1)S(1)} fusion(f32[256,2,128]{2,0,1:T(8,128)} %copy-done.2, f32[256,48,128]{2,0,1:T(8,128)} %copy-done, f32[256,2,128]{2,0,1:T(8,128)S(1)} %collective-permute-done), kind=kLoop, calls=%fused_computation.36 | loop fusion | flops 17301504 | bytes 9961472 | tf_op jit(solution)/shard_map/stack | solution.py:41
  64.6 5.0 %copy.17 = f32[256,52,2]{2,0,1:T(8,128)} copy(f32[256,52,2]{0,2,1:T(2,128)} %collective-permute-done.2) | data formatting | bytes 212992 | tf_op jit(solution)/shard_map/ppermute | solution.py:15
  69.6 5.1 %copy.19 = f32[256,52,2]{2,0,1:T(8,128)} copy(f32[256,52,2]{0,2,1:T(2,128)} %collective-permute-done.3) | data formatting | bytes 212992 | tf_op jit(solution)/shard_map/ppermute | solution.py:17
  74.7 21.3 %fusion.18 = bf16[256,1,48,128]{3,0,2,1:T(8,128)(2,1)S(1)} fusion(f32[256,52,2]{2,0,1:T(8,128)} %copy.19, f32[256,2,128]{2,0,1:T(8,128)} %copy-done.2, f32[256,48,128]{2,0,1:T(8,128)} %copy-done, f32[256,2,128]{2,0,1:T(8,128)S(1)} %collective-permute-done, f32[256,52,2]{2,0,1:T(8,128)} %copy.17), kind=kLoop, calls=%fused_computation.37 | loop fusion | flops 29884416 | bytes 10174464 | tf_op jit(solution)/shard_map/stack | solution.py:41
  96.0 1.7 copy-done.1
  97.6 2.5 fusion.20
  100.5 98.4 %all-reduce.5.cloned.1.call-done = f32[256,256]{0,1:T(8,128)} async-done(((f32[256,256]{0,1:T(8,128)}), f32[256,256]{0,1:T(8,128)}) %all-reduce.5.cloned.1.call-update) | async-done | bytes 262160 | tf_op jit(solution)/shard_map/psum | solution.py:57
  199.0 5.9 %fusion.8 = bf16[255,2,48,128]{3,0,2,1:T(8,128)(2,1)} fusion(bf16[256,1,48,128]{3,0,2,1:T(8,128)(2,1)S(1)} %fusion.17, bf16[256,1,48,128]{3,0,2,1:T(8,128)(2,1)} %copy-done.1), kind=kLoop, calls=%fused_computation.17 | loop fusion | flops 3133440 | bytes 12558336 | tf_op jit(solution)/shard_map/stack | solution.py:41
  204.8 8.7 %copy.22 = bf16[255,2,48,128]{0,3,2,1:T(8,128)(2,1)} copy(bf16[255,2,48,128]{3,0,2,1:T(8,128)(2,1)} %fusion.8) | data formatting | bytes 12533760 | tf_op jit(solution)/shard_map/slice | solution.py:63
  213.5 96.0 %all-reduce.7.cloned.1.call-done = f32[256,256]{0,1:T(8,128)} async-done(((f32[256,256]{0,1:T(8,128)}), f32[256,256]{0,1:T(8,128)}) %all-reduce.7.cloned.1.call-update) | async-done | bytes 262160 | tf_op jit(solution)/shard_map/psum | solution.py:57
  309.5 1.1 copy.21
  310.6 1.0 fusion.21
  311.6 11.7 %cholesky.51 = f32[128,128]{1,0:T(8,128)S(1)} custom-call(f32[128,128]{1,0:T(8,128)S(1)} %cholesky.124), custom_call_target="Cholesky" | custom-call | tf_op jit(solution)/shard_map/jit(cholesky)/cholesky | solution.py:58
  323.3 9.8 %custom-call.14 = f32[1,128,128]{1,2,0:T(8,128)S(1)} custom-call(f32[1,128,128]{2,1,0:T(8,128)S(1)} %get-tuple-element.50), custom_call_target="InvertDiagBlocksLowerTriangular" | custom-call | tf_op jit(solution)/shard_map/jit(cholesky)/cholesky | solution.py:58
  333.6 11.6 %cholesky.110 = f32[127,127]{1,0:T(8,128)S(1)} custom-call(f32[127,127]{1,0:T(8,128)S(1)} %convolution_subtract_fusion.3), custom_call_target="Cholesky" | custom-call | tf_op jit(solution)/shard_map/jit(cholesky)/cholesky | solution.py:58
  348.0 19.9 %custom-call.17 = f32[2,128,128]{1,2,0:T(8,128)S(1)} custom-call(f32[2,128,128]{2,1,0:T(8,128)S(1)} %pad_maximum_fusion.15), custom_call_target="InvertDiagBlocksLowerTriangular" | custom-call | tf_op jit(solution)/shard_map/triangular_solve/custom-call.0 | solution.py:25
  368.0 1.2 fusion.25
  369.2 1.3 convolution_subtract_fusion.1
  373.7 4.6 %convolution_convert_fusion = bf16[255,12288]{1,0:T(8,128)(2,1)S(1)} fusion(bf16[255,12288]{0,1:T(8,128)(2,1)} %bitcast.62, bf16[127,255]{1,0:T(8,128)(2,1)S(1)} %fusion.35, f32[128,255]{1,0:T(8,128)S(1)} %fusion.27), kind=kOutput, calls=%fused_computation | convolution fusion | flops 1601447936 | bytes 12729090 | tf_op jit(solution)/shard_map/dot_general | solution.py:63
  378.3 1.5 copy.32
  379.7 3.8 slice.212
  (38 shorter events, 6.2 us)
Async XLA Ops:
  7.2 191.8 %all-reduce.5.cloned.1.call-start = ((), (), s32[]{:S(2)}) async-start(), calls=%async_computation | async-start | bytes 524288 | tf_op jit(solution)/shard_map/psum | solution.py:57
  12.5 6.9 %copy-start = (f32[256,48,128]{2,0,1:T(8,128)}, f32[256,48,128]{2,0,1:T(8,128)S(1)}, u32[]{:S(2)}) copy-start(f32[256,48,128]{2,0,1:T(8,128)S(1)} %divide_bitcast_fusion) | copy-start | bytes 18874372
  12.5 3.1 collective-permute-start
  14.3 5.1 %collective-permute-start.1 = (f32[256,2,128]{2,0,1:T(8,128)S(1)}, f32[256,2,128]{2,0,1:T(8,128)S(1)}, u32[]{:S(2)}, u32[]{:S(2)}) collective-permute-start(f32[256,2,128]{2,0,1:T(8,128)S(1)} %get-tuple-element.44), channel_id=1, source_target_pairs={{16,0},{32,16},{48,32},{64,48},{80,64},{96,80},{112,96},{128,112},... | collective-permute-start | bytes 786440 | tf_op jit(solution)/shard_map/ppermute | solution.py:17
  19.4 0.7 copy-start.2
  40.1 24.5 %collective-permute-start.2 = (f32[256,52,2]{0,2,1:T(2,128)S(1)}, f32[256,52,2]{0,2,1:T(2,128)}, u32[]{:S(2)}, u32[]{:S(2)}) collective-permute-start(f32[256,52,2]{0,2,1:T(2,128)S(1)} %copy.16), channel_id=1, source_target_pairs={{0,1},{1,2},{2,3},{3,4},{4,5},{5,6},{6,7},{7,8},{8,9},{9,10},{10,1... | collective-permute-start | bytes 319496 | tf_op jit(solution)/shard_map/ppermute | solution.py:15
  48.9 20.7 %collective-permute-start.3 = (f32[256,52,2]{0,2,1:T(2,128)}, f32[256,52,2]{0,2,1:T(2,128)}, u32[]{:S(2)}, u32[]{:S(2)}) collective-permute-start(f32[256,52,2]{0,2,1:T(2,128)} %copy.18), channel_id=1, source_target_pairs={{1,0},{2,1},{3,2},{4,3},{5,4},{6,5},{7,6},{8,7},{9,8},{10,9},{11,1... | collective-permute-start | bytes 319496 | tf_op jit(solution)/shard_map/ppermute | solution.py:17
  96.0 1.7 copy-start.1
  100.2 209.3 %all-reduce.7.cloned.1.call-start = ((), (), s32[]{:S(2)}) async-start(), calls=%async_computation.1 | async-start | bytes 524288 | tf_op jit(solution)/shard_map/psum | solution.py:57
  204.8 143.1 %copy-start.3 = (f32[128,1]{1,0:T(8,128)S(1)}, f32[128,1]{1,0:T(8,128)}, u32[]{:S(2)}) copy-start(f32[128,1]{1,0:T(8,128)} %constant.87.clone.3) | copy-start | bytes 1540
Sparse Core Ops, SparseCore 0:
  100.3 98.5 all-reduce.4
  201.3 108.0 all-reduce.6
